TPU v7x, 32 devices: a whole 2x2x4 slice. The times are simulated.
32 devices in a mesh: runs: 2 (over x), tile: 16 (over z, y, core).
Axes of the slice: x: 2, y: 2, z: 4, core: 2. Of those that a mesh axis runs over, the one named last changes fastest.
Arguments:
- fluid_press: float32 [8192, 128], P(('runs', 'tile')), parts along dimension 0, may hold values from -6 to 6
- iterate: float32 [8192, 128], P(('runs', 'tile')), parts along dimension 0, may hold values from -6 to 6
- displace: float32 [4096, 128], P(('runs', 'tile')), parts along dimension 0, may hold values from -6 to 6
- velocity: float32 [4096, 128], P(('runs', 'tile')), parts along dimension 0, may hold values from -6 to 6
- stiffness: float32 [4096, 128], P(('runs', 'tile')), parts along dimension 0, may hold values from 0.08 to 0.45
- owners: int32 [4096, 1], P(('runs', 'tile')), parts along dimension 0, may hold values from 0 to 15; in each aligned block of 128 rows (0 to 127, 128 to 255, ...) at most 16 rows name the same one
- diff_cur: bfloat16 [40, 8192, 128], P(None, ('runs', 'tile')), parts along dimension 1, may hold values from -1.1048543 to 1.1048543
- step_cur: bfloat16 [40, 8192, 128], P(None, ('runs', 'tile')), parts along dimension 1, may hold values from -6 to 6
- diff_past: bfloat16 [30, 8192, 128], P(None, ('runs', 'tile')), parts along dimension 1, may hold values from -1.1048543 to 1.1048543
- step_past: bfloat16 [30, 8192, 128], P(None, ('runs', 'tile')), parts along dimension 1, may hold values from -6 to 6
Outputs:
- new_iterate: float32 [8192, 128], P(('runs', 'tile')), parts along dimension 0
- displace_out: float32 [4096, 128], P(('runs', 'tile')), parts along dimension 0
- velocity_out: float32 [4096, 128], P(('runs', 'tile')), parts along dimension 0
There are 2 independent parts, one for each index of `runs`. A program takes and returns all parts, laid end to end along the dimension named above; each array names one. Nothing has to cross between parts.
Inputs may be any that keep to these rules, and one draw needn't show every extreme that they name: `owners`: in the 128 lines of one device no partition is named more than 16 times; some partition is named exactly 16 times.
All inputs are finite; a program needn't handle non-finite values.
Results may differ from a plain program's by a relative error of at most 0.0042.
Values sent between devices are 32-bit elements; how exact they have to be, the bound alone decides.
No kernel may reach another device: no remote copies, remote signals or barrier semaphores. Data moves between devices by JAX's collectives and lax.ppermute only.
A program may use at most 64 MiB of HBM per device.

v0:
```python
import jax
import jax.numpy as jnp
from jax import lax
from jax.experimental import pallas as pl
from jax.sharding import PartitionSpec as P


SUBSTEPS = 4


step_dt = 1.0
damping = 0.05


def tree_sum(value, axis):
    count = lax.axis_size(axis)
    if count & (count - 1):
        return lax.psum(value, axis)
    stride = 1
    while stride < count:
        value = value + lax.ppermute(value, axis, [(i, i ^ stride) for i in range(count)])
        stride *= 2
    return value


def halo_pair(cells, width, axis):
    count = lax.axis_size(axis)
    below = lax.ppermute(cells[-width:], axis, [(i, (i + 1) % count) for i in range(count)])
    above = lax.ppermute(cells[:width], axis, [((i + 1) % count, i) for i in range(count)])
    return below, above


def to_half(value):
    return lax.reduce_precision(value, exponent_bits=8, mantissa_bits=7)


def sides(center):
    zero_col = jnp.zeros((center.shape[0], 1), jnp.float32)
    left = jnp.concatenate([zero_col, center[:, :-1]], 1)
    right = jnp.concatenate([center[:, 1:], zero_col], 1)
    return left + right


def eliminate(mats):
    state = []
    for a in mats:
        n = a.shape[0]
        rows = lax.broadcasted_iota(jnp.int32, (n, n), 0)
        cols = lax.broadcasted_iota(jnp.int32, (n, n), 1)
        state.append([a, jnp.where(rows == cols, 1.0, 0.0).astype(jnp.float32), rows, cols])
    for j in range(max(a.shape[0] for a in mats)):
        for item in state:
            a, m, rows, cols = item
            if j >= a.shape[0]:
                continue
            on_row = rows == j
            row = jnp.sum(jnp.where(on_row, a, 0.0), axis=0, keepdims=True)
            col = jnp.sum(jnp.where(cols == j, a, 0.0), axis=1, keepdims=True)
            pivot = jnp.sum(jnp.where(cols[:1] == j, row, 0.0), axis=1, keepdims=True)
            scale = 1.0 / jnp.sqrt(pivot)
            row = jnp.where(cols[:1] >= j, row * scale, 0.0)
            lower = jnp.where(rows[:, :1] > j, col * scale, 0.0)
            m_row = jnp.sum(jnp.where(on_row, m, 0.0), axis=0, keepdims=True) * scale
            item[0] = jnp.where(on_row, row, a - lower * row)
            item[1] = jnp.where(on_row, m_row, m - lower * m_row)
    return [item[1] for item in state]


def as_column(row):
    n = row.shape[1]
    eye = lax.broadcasted_iota(jnp.int32, (n, n), 0) == lax.broadcasted_iota(jnp.int32, (n, n), 1)
    return jnp.sum(jnp.where(eye, row, 0.0), axis=1, keepdims=True)


def as_row(col):
    n = col.shape[0]
    eye = lax.broadcasted_iota(jnp.int32, (n, n), 0) == lax.broadcasted_iota(jnp.int32, (n, n), 1)
    return jnp.sum(jnp.where(eye, col, 0.0), axis=0, keepdims=True)


def solve_kernel(sums_ref, coeff_ref, past_ref):
    n_cur = coeff_ref.shape[1]
    n_all = sums_ref.shape[1]
    sums = sums_ref[...]
    gram_cur = sums[:n_cur, :n_cur]
    gram_past = sums[n_cur:n_all, n_cur:n_all]
    cross = sums[n_cur:n_all, :n_cur]
    rhs_cur = sums[n_all:, :n_cur]
    rhs_past = sums[n_all:, n_cur:n_all]
    inv_cur, inv_past = eliminate([gram_cur, gram_past])
    inner = jnp.sum(inv_cur * rhs_cur, axis=1, keepdims=True)
    coeff = -jnp.sum(inv_cur * inner, axis=0, keepdims=True)
    projected = as_column(rhs_past) + jnp.sum(cross * coeff, axis=1, keepdims=True)
    inner = jnp.sum(inv_past * as_row(projected), axis=1, keepdims=True)
    coeff_ref[...] = coeff
    past_ref[...] = jnp.sum(inv_past * inner, axis=0, keepdims=True)


def solve_both(sums, n_cur):
    n_past = sums.shape[1] - n_cur
    shapes = (jax.ShapeDtypeStruct((1, n_cur), jnp.float32), jax.ShapeDtypeStruct((1, n_past), jnp.float32))
    coeff, past = pl.pallas_call(solve_kernel, out_shape=shapes)(sums)
    return coeff[0], past[0]


def body(
    fluid_press,
    iterate,
    displace,
    velocity,
    stiffness,
    owners,
    diff_cur,
    step_cur,
    diff_past,
    step_past,
):
    high = lax.Precision.HIGHEST
    tile_count = lax.axis_size("tile")
    line_count = displace.shape[0]
    slot_count = iterate.shape[0]
    per_pair = slot_count // tile_count
    n_cur = diff_cur.shape[0]
    owner_list = owners[:, 0]
    onehot = (owner_list[:, None] == jnp.arange(tile_count, dtype=jnp.int32)[None, :]).astype(
        jnp.float32
    )
    below = (jnp.arange(line_count)[:, None] > jnp.arange(line_count)[None, :]).astype(jnp.float32)
    earlier = jnp.dot(below, onehot, precision=high)
    rank_in = jnp.sum(earlier * onehot, axis=1).astype(jnp.int32)
    slot_of = owner_list * per_pair + rank_in
    chooser = (slot_of[:, None] == jnp.arange(slot_count, dtype=jnp.int32)[None, :]).astype(
        jnp.float32
    )
    flags = jnp.sum(chooser, axis=0)
    lanes = fluid_press.shape[1]
    width = SUBSTEPS

    edge = jnp.concatenate([displace, velocity, stiffness], axis=1)
    edge_below, edge_above = halo_pair(edge, width, "tile")

    flag_rows = jnp.zeros((tile_count, 1, lanes), jnp.float32)
    flag_rows = flag_rows.at[:, 0, :per_pair].set(flags.reshape(tile_count, per_pair))
    sent = jnp.concatenate([fluid_press.reshape(tile_count, per_pair, lanes), flag_rows], axis=1)
    got = lax.all_to_all(sent, "tile", split_axis=0, concat_axis=0, tiled=True)
    returned = got[:, :per_pair, :].reshape(slot_count, lanes)
    mask = got[:, per_pair, :per_pair].reshape(slot_count)
    mask_half = mask.astype(jnp.bfloat16)

    cols = jnp.concatenate(
        [
            (diff_cur * mask_half[None, :, None]).reshape(n_cur, -1),
            (diff_past * mask_half[None, :, None]).reshape(diff_past.shape[0], -1),
        ],
        axis=0,
    )
    gram = lax.dot_general(cols, cols, (((1,), (1,)), ((), ())), preferred_element_type=jnp.float32)

    pressure = jnp.dot(chooser, returned, precision=high)
    press_below, press_above = halo_pair(pressure, width, "tile")
    packed = jnp.concatenate(
        [
            jnp.concatenate([edge_below, press_below], axis=1),
            jnp.concatenate([edge, pressure], axis=1),
            jnp.concatenate([edge_above, press_above], axis=1),
        ],
        axis=0,
    )
    field = packed[:, :lanes]
    speed = packed[:, lanes : 2 * lanes]
    stiff = packed[:, 2 * lanes : 3 * lanes]
    press = packed[:, 3 * lanes :]
    for _ in range(SUBSTEPS):
        lapl = jnp.roll(field, 1, 0) + jnp.roll(field, -1, 0) + sides(field) - 4.0 * field
        speed = speed + step_dt * (stiff * lapl + press - damping * speed)
        field = field + step_dt * speed
    field = field[width : width + line_count]
    speed = speed[width : width + line_count]

    outgoing = jnp.dot(chooser.T, field, precision=high)
    x_tilde = lax.all_to_all(outgoing, "tile", split_axis=0, concat_axis=0, tiled=True)
    resid = to_half(mask[:, None] * (x_tilde - iterate))
    inner = jnp.concatenate(
        [
            jnp.sum(diff_cur.astype(jnp.float32) * resid[None], axis=(1, 2)),
            jnp.sum(diff_past.astype(jnp.float32) * resid[None], axis=(1, 2)),
        ]
    )
    summed = tree_sum(jnp.concatenate([gram, inner[None]], axis=0), "tile")
    coeff, past = solve_both(summed, n_cur)
    coeff_half = to_half(coeff)
    past_half = to_half(past)
    upd_cur = jnp.sum(coeff_half[:, None, None] * step_cur.astype(jnp.float32), axis=0)
    upd_past = jnp.sum(past_half[:, None, None] * step_past.astype(jnp.float32), axis=0)
    update = upd_cur - upd_past
    new_iterate = mask[:, None] * (x_tilde + update)
    return (new_iterate, field, speed)


def solution(mesh):
    placed = (
        P(("runs", "tile"), None),
        P(("runs", "tile"), None),
        P(("runs", "tile"), None),
        P(("runs", "tile"), None),
        P(("runs", "tile"), None),
        P(("runs", "tile"), None),
        P(None, ("runs", "tile"), None),
        P(None, ("runs", "tile"), None),
        P(None, ("runs", "tile"), None),
        P(None, ("runs", "tile"), None),
    )
    return jax.shard_map(
        body,
        mesh=mesh,
        in_specs=placed,
        out_specs=(P(("runs", "tile"), None), P(("runs", "tile"), None), P(("runs", "tile"), None)),
        check_vma=False,
    )
```

profile of v0, /device:TPU:0, one launch (start us, length us, event | category | flops | bytes accessed | tf_op | source)
XLA Modules:
  0.0 76.9 jit_solution(14756268758769805380)
XLA Ops:
  0.6 0.9 %fusion.4 = f32[128]{0:T(128)S(1)} fusion(s32[128]{0:T(128)} %bitcast.40), kind=kOutput, calls=%fused_computation.11 | convolution fusion | flops 548736 | bytes 1024 | tf_op jit(solution)/shard_map/dot_general | solution.py:129
  1.5 0.7 fusion.37
  2.2 0.1 convert_reduce_fusion
  2.3 0.1 reshape.89
  2.4 1.6 %select_maximum_fusion = f32[16,17,128]{2,1,0:T(8,128)} fusion(f32[16,1,16]{2,1,0:T(1,128)S(1)} %reshape.89, f32[16,16,128]{2,1,0:T(8,128)} %bitcast.39), kind=kLoop, calls=%fused_computation.14 | loop fusion | flops 104448 | bytes 271360 | tf_op jit(solution)/shard_map/concatenate | solution.py:144
  4.0 7.4 %all-to-all-start = ((f32[16,17,128]{2,1,0:T(8,128)}), f32[16,17,128]{2,1,0:T(8,128)S(1)}, u32[]{:S(2)}, u32[]{:S(2)}) async-start(f32[16,17,128]{2,1,0:T(8,128)} %select_maximum_fusion), calls=%async_computation | async-start | bytes 393216 | tf_op jit(solution)/shard_map/all_to_all | solution.py:145
  11.4 0.8 %constant_dynamic-update-slice_fusion.2 = f32[128,384]{1,0:T(8,128)S(1)} fusion(f32[128,128]{1,0:T(8,128)} %param.14), kind=kLoop, calls=%fused_computation.62 | loop fusion | bytes 131072
  12.3 0.8 %constant_dynamic-update-slice_fusion.1 = f32[128,384]{1,0:T(8,128)S(1)} fusion(f32[128,384]{1,0:T(8,128)S(1)} %constant_dynamic-update-slice_fusion.2, f32[128,128]{1,0:T(8,128)} %param.15), kind=kLoop, calls=%fused_computation.61 | loop fusion | bytes 131072
  13.1 0.8 %constant_dynamic-update-slice_fusion = f32[128,384]{1,0:T(8,128)S(1)} fusion(f32[128,384]{1,0:T(8,128)S(1)} %constant_dynamic-update-slice_fusion.1, f32[128,128]{1,0:T(8,128)} %param.16), kind=kLoop, calls=%fused_computation.60 | loop fusion | bytes 131072 | tf_op jit(solution)/shard_map/concatenate | solution.py:139
  13.9 0.5 collective-permute-start
  14.4 4.0 %collective-permute-start.2 = (f32[4,384]{1,0:T(4,128)S(1)}, f32[4,384]{1,0:T(4,128)S(1)}, u32[]{:S(2)}, u32[]{:S(2)}) collective-permute-start(f32[4,384]{1,0:T(4,128)S(1)} %get-tuple-element.32), channel_id=1, source_target_pairs={{1,0},{2,1},{3,2},{4,3},{5,4},{6,5},{7,6},{8,7},{9,8},{10,9},{11,1... | collective-permute-start | bytes 18440 | tf_op jit(solution)/shard_map/ppermute | solution.py:29
  18.4 1.5 %collective-permute-done = f32[4,384]{1,0:T(4,128)S(1)} collective-permute-done((f32[4,384]{1,0:T(4,128)S(1)}, f32[4,384]{1,0:T(4,128)S(1)}, u32[]{:S(2)}, u32[]{:S(2)}) %collective-permute-start) | collective-permute-done | bytes 6176 | tf_op jit(solution)/shard_map/ppermute | solution.py:28
  19.9 0.5 all-to-all-done
  20.5 0.1 mul.113
  20.6 0.3 fusion.9
  20.9 4.4 %collective-permute-start.3 = (f32[4,128]{1,0:T(4,128)S(1)}, f32[4,128]{1,0:T(4,128)S(1)}, u32[]{:S(2)}, u32[]{:S(2)}) collective-permute-start(f32[4,128]{1,0:T(4,128)S(1)} %get-tuple-element.52), channel_id=1, source_target_pairs={{1,0},{2,1},{3,2},{4,3},{5,4},{6,5},{7,6},{8,7},{9,8},{10,9},{11,1... | collective-permute-start | bytes 6152 | tf_op jit(solution)/shard_map/ppermute | solution.py:29
  25.3 2.0 %broadcast_multiply_fusion = bf16[40,256,128]{2,1,0:T(8,128)(2,1)S(1)} fusion(bf16[40,256,128]{2,1,0:T(8,128)(2,1)} %param.18, bf16[256]{0:T(256)(128)(2,1)S(1)} %convert_element_type.40), kind=kLoop, calls=%fused_computation.9 | loop fusion | flops 1310720 | bytes 5243392 | tf_op jit(solution)/shard_map/mul | solution.py:152
  27.3 0.2 broadcast_multiply_fusion.1
  27.6 0.3 pad.46
  27.9 2.7 %copy.14 = bf16[4,8,256,128]{3,1,2,0:T(8,128)(2,1)} copy(bf16[4,8,256,128]{3,2,1,0:T(8,128)(2,1)S(1)} %bitcast.35) | data formatting | bytes 4194304
  30.6 3.2 %copy.16 = bf16[5,8,256,128]{3,1,2,0:T(8,128)(2,1)} copy(bf16[5,8,256,128]{3,2,1,0:T(8,128)(2,1)S(1)} %bitcast.34) | data formatting | bytes 5242880
  33.8 0.1 fusion.45
  33.9 0.1 slice_add_fusion.1
  34.0 0.1 fusion.55
  34.1 0.1 fusion.41
  34.3 0.1 fusion.52
  34.4 0.1 fusion.39
  34.6 0.1 fusion.33
  34.7 0.6 slice_add_fusion
  35.4 1.0 %fusion.8 = f32[256,128]{1,0:T(8,128)} fusion(f32[128,128]{1,0:T(8,128)S(1)} %get-tuple-element.19, s32[128]{0:T(128)S(1)} %fusion.37), kind=kOutput, calls=%fused_computation.23 | convolution fusion | flops 50364416 | bytes 197120 | tf_op jit(solution)/shard_map/dot_general | solution.py:180
  36.4 3.5 %all-to-all-start.1 = ((f32[16,16,128]{2,1,0:T(8,128)}), f32[16,16,128]{2,1,0:T(8,128)S(1)}, u32[]{:S(2)}, u32[]{:S(2)}) async-start(f32[16,16,128]{2,1,0:T(8,128)} %bitcast.5), calls=%async_computation.1 | async-start | bytes 262144 | tf_op jit(solution)/shard_map/all_to_all | solution.py:181
  39.9 5.3 %fusion = f32[70,70]{1,0:T(8,128)S(1)} fusion(bf16[30,32768]{1,0:T(8,128)(2,1)} %bitcast.37, bf16[40,32768]{1,0:T(8,128)(2,1)} %bitcast.36), kind=kOutput, calls=%fused_computation.2 | convolution fusion | flops 330301440 | bytes 4607120 | tf_op jit(solution)/shard_map/dot_general | solution.py:157
  45.2 2.5 %all-to-all-done.1 = f32[16,16,128]{2,1,0:T(8,128)S(1)} async-done(((f32[16,16,128]{2,1,0:T(8,128)}), f32[16,16,128]{2,1,0:T(8,128)S(1)}, u32[]{:S(2)}, u32[]{:S(2)}) %all-to-all-start.1) | async-done | bytes 131104 | tf_op jit(solution)/shard_map/all_to_all | solution.py:181
  47.8 0.1 fusion.6
  47.9 2.2 %multiply_reduce_fusion.3 = f32[30]{0:T(128)S(1)} fusion(bf16[30,256,128]{2,1,0:T(8,128)(2,1)} %param.20, f32[256,128]{1,0:T(8,128)S(1)} %fusion.6), kind=kLoop, calls=%fused_computation.7 | loop fusion | flops 2949090 | bytes 2097272 | tf_op jit(solution)/shard_map/reduce_sum | solution.py:186
  50.1 0.8 %multiply_reduce_fusion.1 = f32[40]{0:T(128)S(1)} fusion(bf16[40,256,128]{2,1,0:T(8,128)(2,1)S(1)} %copy-done, f32[256,128]{1,0:T(8,128)S(1)} %fusion.6), kind=kLoop, calls=%fused_computation.1 | loop fusion | flops 3932120 | bytes 2752672 | tf_op jit(solution)/shard_map/reduce_sum | solution.py:185
  51.1 1.2 %collective-permute-done.4 = f32[71,70]{1,0:T(8,128)S(1)} collective-permute-done((f32[71,70]{1,0:T(8,128)S(1)}, f32[71,70]{1,0:T(8,128)S(1)}, u32[]{:S(2)}, u32[]{:S(2)}) %collective-permute-start.4) | collective-permute-done | bytes 19912 | tf_op jit(solution)/shard_map/ppermute | solution.py:21
  52.4 3.9 %collective-permute-done.5 = f32[71,70]{1,0:T(8,128)S(1)} collective-permute-done((f32[71,70]{1,0:T(8,128)S(1)}, f32[71,70]{1,0:T(8,128)S(1)}, u32[]{:S(2)}, u32[]{:S(2)}) %collective-permute-start.5) | collective-permute-done | bytes 19912 | tf_op jit(solution)/shard_map/ppermute | solution.py:21
  56.3 3.9 %collective-permute-done.6 = f32[71,70]{1,0:T(8,128)S(1)} collective-permute-done((f32[71,70]{1,0:T(8,128)S(1)}, f32[71,70]{1,0:T(8,128)S(1)}, u32[]{:S(2)}, u32[]{:S(2)}) %collective-permute-start.6) | collective-permute-done | bytes 19912 | tf_op jit(solution)/shard_map/ppermute | solution.py:21
  60.3 0.3 collective-permute-start.7
  60.6 4.5 %collective-permute-done.7 = f32[71,70]{1,0:T(8,128)S(1)} collective-permute-done((f32[71,70]{1,0:T(8,128)S(1)}, f32[71,70]{1,0:T(8,128)S(1)}, u32[]{:S(2)}, u32[]{:S(2)}) %collective-permute-start.7) | collective-permute-done | bytes 19912 | tf_op jit(solution)/shard_map/ppermute | solution.py:21
  65.2 0.6 add.139.sums_ref
  65.8 6.3 %shard_map.121 = (f32[1,40]{1,0:T(1,128)}, f32[1,30]{1,0:T(1,128)}) custom-call(f32[71,70]{1,0:T(8,128)} %add.139.sums_ref), custom_call_target="tpu_custom_call" | custom-call | tf_op jit(solution)/shard_map/pallas_call | solution.py:102
  72.1 0.6 reduce-precision_bitcast_fusion.1
  72.6 0.7 reduce-precision_bitcast_fusion
  73.3 2.0 %multiply_reduce_fusion.2 = f32[256,128]{1,0:T(8,128)S(1)} fusion(bf16[30,256,128]{2,1,0:T(8,128)(2,1)} %param.21, f32[30]{0:T(128)S(1)} %reduce-precision_bitcast_fusion), kind=kLoop, calls=%fused_computation.6 | loop fusion | flops 2916352 | bytes 2097272 | tf_op jit(solution)/shard_map/reduce_sum | solution.py:194
  75.3 0.8 multiply_reduce_fusion
  76.1 0.8 fusion.7
  (44 shorter events, 0.6 us)
Async XLA Ops:
  4.0 16.4 %all-to-all-start = ((f32[16,17,128]{2,1,0:T(8,128)}), f32[16,17,128]{2,1,0:T(8,128)S(1)}, u32[]{:S(2)}, u32[]{:S(2)}) async-start(f32[16,17,128]{2,1,0:T(8,128)} %select_maximum_fusion), calls=%async_computation | async-start | bytes 393216 | tf_op jit(solution)/shard_map/all_to_all | solution.py:145
  13.9 6.0 %collective-permute-start = (f32[4,384]{1,0:T(4,128)S(1)}, f32[4,384]{1,0:T(4,128)S(1)}, u32[]{:S(2)}, u32[]{:S(2)}) collective-permute-start(f32[4,384]{1,0:T(4,128)S(1)} %get-tuple-element.31), channel_id=1, source_target_pairs={{0,1},{1,2},{2,3},{3,4},{4,5},{5,6},{6,7},{7,8},{8,9},{9,10},{10,1... | collective-permute-start | bytes 18440 | tf_op jit(solution)/shard_map/ppermute | solution.py:28
  14.4 5.5 %collective-permute-start.2 = (f32[4,384]{1,0:T(4,128)S(1)}, f32[4,384]{1,0:T(4,128)S(1)}, u32[]{:S(2)}, u32[]{:S(2)}) collective-permute-start(f32[4,384]{1,0:T(4,128)S(1)} %get-tuple-element.32), channel_id=1, source_target_pairs={{1,0},{2,1},{3,2},{4,3},{5,4},{6,5},{7,6},{8,7},{9,8},{10,9},{11,1... | collective-permute-start | bytes 18440 | tf_op jit(solution)/shard_map/ppermute | solution.py:29
  20.8 12.9 %collective-permute-start.1 = (f32[4,128]{1,0:T(4,128)S(1)}, f32[4,128]{1,0:T(4,128)S(1)}, u32[]{:S(2)}, u32[]{:S(2)}) collective-permute-start(f32[4,128]{1,0:T(4,128)S(1)} %get-tuple-element.51), channel_id=1, source_target_pairs={{0,1},{1,2},{2,3},{3,4},{4,5},{5,6},{6,7},{7,8},{8,9},{9,10},{10,1... | collective-permute-start | bytes 6152 | tf_op jit(solution)/shard_map/ppermute | solution.py:28
  20.9 6.4 %copy-start.1 = (bf16[30,256,128]{2,1,0:T(8,128)(2,1)S(1)}, bf16[30,256,128]{2,1,0:T(8,128)(2,1)}, u32[]{:S(2)}) copy-start(bf16[30,256,128]{2,1,0:T(8,128)(2,1)} %param.20) | copy-start | bytes 5898244
  20.9 12.8 %collective-permute-start.3 = (f32[4,128]{1,0:T(4,128)S(1)}, f32[4,128]{1,0:T(4,128)S(1)}, u32[]{:S(2)}, u32[]{:S(2)}) collective-permute-start(f32[4,128]{1,0:T(4,128)S(1)} %get-tuple-element.52), channel_id=1, source_target_pairs={{1,0},{2,1},{3,2},{4,3},{5,4},{6,5},{7,6},{8,7},{9,8},{10,9},{11,1... | collective-permute-start | bytes 6152 | tf_op jit(solution)/shard_map/ppermute | solution.py:29
  30.6 3.2 %copy-start.3 = (f32[128,128]{1,0:T(8,128)S(1)}, f32[128,128]{1,0:T(8,128)}, u32[]{:S(2)}) copy-start(f32[128,128]{1,0:T(8,128)} %param.14) | copy-start | bytes 196612
  30.6 3.2 %copy-start.4 = (f32[128,128]{1,0:T(8,128)S(1)}, f32[128,128]{1,0:T(8,128)}, u32[]{:S(2)}) copy-start(f32[128,128]{1,0:T(8,128)} %param.15) | copy-start | bytes 196612
  30.6 3.2 %copy-start.5 = (f32[128,128]{1,0:T(8,128)S(1)}, f32[128,128]{1,0:T(8,128)}, u32[]{:S(2)}) copy-start(f32[128,128]{1,0:T(8,128)} %param.16) | copy-start | bytes 196612
  35.4 9.9 %copy-start.6 = (f32[128,128]{1,0:T(8,128)}, f32[128,128]{1,0:T(8,128)S(1)}, u32[]{:S(2)}) copy-start(f32[128,128]{1,0:T(8,128)S(1)} %get-tuple-element.19) | copy-start | bytes 196612
  36.4 11.4 %all-to-all-start.1 = ((f32[16,16,128]{2,1,0:T(8,128)}), f32[16,16,128]{2,1,0:T(8,128)S(1)}, u32[]{:S(2)}, u32[]{:S(2)}) async-start(f32[16,16,128]{2,1,0:T(8,128)} %bitcast.5), calls=%async_computation.1 | async-start | bytes 262144 | tf_op jit(solution)/shard_map/all_to_all | solution.py:181
  39.9 7.9 %copy-start.7 = (f32[256,128]{1,0:T(8,128)S(1)}, f32[256,128]{1,0:T(8,128)}, u32[]{:S(2)}) copy-start(f32[256,128]{1,0:T(8,128)} %param.13) | copy-start | bytes 393220
  39.9 10.2 %copy-start = (bf16[40,256,128]{2,1,0:T(8,128)(2,1)S(1)}, bf16[40,256,128]{2,1,0:T(8,128)(2,1)}, u32[]{:S(2)}) copy-start(bf16[40,256,128]{2,1,0:T(8,128)(2,1)} %param.18) | copy-start | bytes 7864324
  50.9 24.4 %copy-start.2 = (bf16[40,256,128]{2,1,0:T(8,128)(2,1)S(1)}, bf16[40,256,128]{2,1,0:T(8,128)(2,1)}, u32[]{:S(2)}) copy-start(bf16[40,256,128]{2,1,0:T(8,128)(2,1)} %param.19) | copy-start | bytes 7864324
  51.0 1.3 %collective-permute-start.4 = (f32[71,70]{1,0:T(8,128)S(1)}, f32[71,70]{1,0:T(8,128)S(1)}, u32[]{:S(2)}, u32[]{:S(2)}) collective-permute-start(f32[71,70]{1,0:T(8,128)S(1)} %pad_maximum_fusion), channel_id=1, source_target_pairs={{0,1},{1,0},{2,3},{3,2},{4,5},{5,4},{6,7},{7,6},{8,9},{9,8},{10,11... | collective-permute-start | bytes 59648 | tf_op jit(solution)/shard_map/ppermute | solution.py:21
  52.3 4.0 %collective-permute-start.5 = (f32[71,70]{1,0:T(8,128)S(1)}, f32[71,70]{1,0:T(8,128)S(1)}, u32[]{:S(2)}, u32[]{:S(2)}) collective-permute-start(f32[71,70]{1,0:T(8,128)S(1)} %fusion.59), channel_id=1, source_target_pairs={{0,2},{1,3},{2,0},{3,1},{4,6},{5,7},{6,4},{7,5},{8,10},{9,11},{10,... | collective-permute-start | bytes 59648 | tf_op jit(solution)/shard_map/ppermute | solution.py:21
  56.3 4.0 %collective-permute-start.6 = (f32[71,70]{1,0:T(8,128)S(1)}, f32[71,70]{1,0:T(8,128)S(1)}, u32[]{:S(2)}, u32[]{:S(2)}) collective-permute-start(f32[71,70]{1,0:T(8,128)S(1)} %add.137), channel_id=1, source_target_pairs={{0,4},{1,5},{2,6},{3,7},{4,0},{5,1},{6,2},{7,3},{8,12},{9,13},{10,... | collective-permute-start | bytes 59648 | tf_op jit(solution)/shard_map/ppermute | solution.py:21
  60.3 4.9 %collective-permute-start.7 = (f32[71,70]{1,0:T(8,128)S(1)}, f32[71,70]{1,0:T(8,128)S(1)}, u32[]{:S(2)}, u32[]{:S(2)}) collective-permute-start(f32[71,70]{1,0:T(8,128)S(1)} %add.138), channel_id=1, source_target_pairs={{0,8},{1,9},{2,10},{3,11},{4,12},{5,13},{6,14},{7,15},{8,0},{9,1},... | collective-permute-start | bytes 59648 | tf_op jit(solution)/shard_map/ppermute | solution.py:21
where the time goes:
time: 77.5 us; the launch traced here: 76.9 us
  starting transfers between devices  20.4 us (26%)
  waiting for transfers between devices  18.2 us (23%)
  other arithmetic  14.3 us (18%)
  local copies, waits for them, and re-layouts  9.36 us (12%)
  matrix products  7.43 us (10%)
  Pallas kernels  6.28 us (8%)
  between operations  0.92 us (1%)
    ppermute x4, waiting for transfers between devices, tree_sum(): lax.ppermute(value, axis, [(i, i ^ stride) for i in range(count)])  13.6 us
    ppermute x2, starting transfers between devices, halo_pair(): lax.ppermute(cells[:width], axis, [((i + 1) % count, i) for i in range(co...  8.46 us
    unnamed x21, local copies, waits for them, and re-layouts  7.89 us
    all_to_all x1, starting transfers between devices, body(): got = lax.all_to_all(sent, 'tile', split_axis=0, concat_axis=0, tiled=True)  7.41 us
    pallas_call x1, Pallas kernels, solve_both(): coeff, past = pl.pallas_call(solve_kernel, out_shape=shapes)(sums)  6.28 us
    dot_general x1, matrix products, body(): lax.dot_general(cols, cols, (((1,), (1,)), ((), ())), preferred_element_t...  5.29 us
    all_to_all x1, starting transfers between devices, body(): lax.all_to_all(outgoing, 'tile', split_axis=0, concat_axis=0, tiled=True)  3.51 us
    all_to_all x1, waiting for transfers between devices, body(): lax.all_to_all(outgoing, 'tile', split_axis=0, concat_axis=0, tiled=True)  2.54 us
  transfers between devices with their start and end apart: 10, of which 7 were waited for; matrix products, arithmetic and copies ran while one was open for 21% of the time, Pallas kernels for 0%

commit v1 on v0

--- a/solution.py
+++ b/solution.py
@@ -132,15 +132,17 @@
     chooser = (slot_of[:, None] == jnp.arange(slot_count, dtype=jnp.int32)[None, :]).astype(
         jnp.float32
     )
-    flags = jnp.sum(chooser, axis=0)
+    counts = jnp.sum(onehot, axis=0)
+    flags = (jnp.arange(per_pair, dtype=jnp.float32)[None, :] < counts[:, None]).astype(jnp.float32)
     lanes = fluid_press.shape[1]
     width = SUBSTEPS
 
     edge = jnp.concatenate([displace, velocity, stiffness], axis=1)
     edge_below, edge_above = halo_pair(edge, width, "tile")
 
-    flag_rows = jnp.zeros((tile_count, 1, lanes), jnp.float32)
-    flag_rows = flag_rows.at[:, 0, :per_pair].set(flags.reshape(tile_count, per_pair))
+    flag_count = 8 - per_pair % 8
+    flag_rows = jnp.zeros((tile_count, flag_count, lanes), jnp.float32)
+    flag_rows = flag_rows.at[:, 0, :per_pair].set(flags)
     sent = jnp.concatenate([fluid_press.reshape(tile_count, per_pair, lanes), flag_rows], axis=1)
     got = lax.all_to_all(sent, "tile", split_axis=0, concat_axis=0, tiled=True)
     returned = got[:, :per_pair, :].reshape(slot_count, lanes)

time: 77.5 us -> 76.6 us (0.988)
  waiting for transfers between devices: 18.2 us -> 16.6 us
  other arithmetic: 14.3 us -> 15.1 us
    ppermute x2, waiting for transfers between devices: 1.48 us -> 0.01 us  [halo_pair(): lax.ppermute(cells[-width:], axis, [(i, (i + 1) % count) for i in range(c...]
  transfers between devices with their start and end apart: 10 -> 10, of which waited for: 7 -> 6; matrix products, arithmetic and copies ran while one was open for 21% -> 23% of each run, Pallas kernels for 0% -> 0%
where the time goes in v1:
time: 76.6 us; the launch traced here: 76 us
  starting transfers between devices  20.4 us (27%)
  waiting for transfers between devices  16.6 us (22%)
  other arithmetic  15.1 us (20%)
  local copies, waits for them, and re-layouts  9.27 us (12%)
  matrix products  7.43 us (10%)
  Pallas kernels  6.28 us (8%)
  between operations  0.93 us (1%)
    ppermute x4, waiting for transfers between devices, tree_sum(): lax.ppermute(value, axis, [(i, i ^ stride) for i in range(count)])  13.6 us
    ppermute x2, starting transfers between devices, halo_pair(): lax.ppermute(cells[:width], axis, [((i + 1) % count, i) for i in range(co...  8.46 us
    unnamed x21, local copies, waits for them, and re-layouts  7.89 us
    all_to_all x1, starting transfers between devices, body(): got = lax.all_to_all(sent, 'tile', split_axis=0, concat_axis=0, tiled=True)  7.41 us
    pallas_call x1, Pallas kernels, solve_both(): coeff, past = pl.pallas_call(solve_kernel, out_shape=shapes)(sums)  6.28 us
    dot_general x1, matrix products, body(): lax.dot_general(cols, cols, (((1,), (1,)), ((), ())), preferred_element_t...  5.29 us
    all_to_all x1, starting transfers between devices, body(): lax.all_to_all(outgoing, 'tile', split_axis=0, concat_axis=0, tiled=True)  3.51 us
    all_to_all x1, waiting for transfers between devices, body(): lax.all_to_all(outgoing, 'tile', split_axis=0, concat_axis=0, tiled=True)  2.54 us
  transfers between devices with their start and end apart: 10, of which 6 were waited for; matrix products, arithmetic and copies ran while one was open for 23% of the time, Pallas kernels for 0%

profile of v1, /device:TPU:0, one launch (start us, length us, event | category | flops | bytes accessed | tf_op | source)
XLA Modules:
  0.0 76.0 jit_solution(7032975671208600676)
XLA Ops:
  0.6 0.8 %convert_reduce_fusion = f32[16]{0:T(128)S(1)} fusion(s32[128]{0:T(128)} %bitcast.40), kind=kLoop, calls=%fused_computation.62 | loop fusion | flops 6128 | bytes 576 | tf_op jit(solution)/shard_map/reduce_sum | solution.py:135
  1.4 0.1 iota_compare_fusion.7
  1.5 1.6 %pad_maximum_fusion = f32[16,24,128]{2,1,0:T(8,128)} fusion(f32[16,8,128]{2,1,0:T(8,128)S(1)} %pad_convert_fusion, f32[16,16,128]{2,1,0:T(8,128)} %bitcast.39), kind=kLoop, calls=%fused_computation.14 | loop fusion | flops 49152 | bytes 393216 | tf_op jit(solution)/shard_map/concatenate | solution.py:146
  3.1 7.4 %all-to-all-start = ((f32[16,24,128]{2,1,0:T(8,128)}), f32[16,24,128]{2,1,0:T(8,128)S(1)}, u32[]{:S(2)}, u32[]{:S(2)}) async-start(f32[16,24,128]{2,1,0:T(8,128)} %pad_maximum_fusion), calls=%async_computation | async-start | bytes 393216 | tf_op jit(solution)/shard_map/all_to_all | solution.py:147
  10.5 0.8 %constant_dynamic-update-slice_fusion.2 = f32[128,384]{1,0:T(8,128)S(1)} fusion(f32[128,128]{1,0:T(8,128)} %param.14), kind=kLoop, calls=%fused_computation.61 | loop fusion | bytes 131072
  11.4 0.8 %constant_dynamic-update-slice_fusion.1 = f32[128,384]{1,0:T(8,128)S(1)} fusion(f32[128,384]{1,0:T(8,128)S(1)} %constant_dynamic-update-slice_fusion.2, f32[128,128]{1,0:T(8,128)} %param.15), kind=kLoop, calls=%fused_computation.60 | loop fusion | bytes 131072
  12.2 0.8 %constant_dynamic-update-slice_fusion = f32[128,384]{1,0:T(8,128)S(1)} fusion(f32[128,384]{1,0:T(8,128)S(1)} %constant_dynamic-update-slice_fusion.1, f32[128,128]{1,0:T(8,128)} %param.16), kind=kLoop, calls=%fused_computation.59 | loop fusion | bytes 131072 | tf_op jit(solution)/shard_map/concatenate | solution.py:140
  13.1 0.5 collective-permute-start
  13.5 4.0 %collective-permute-start.2 = (f32[4,384]{1,0:T(4,128)S(1)}, f32[4,384]{1,0:T(4,128)S(1)}, u32[]{:S(2)}, u32[]{:S(2)}) collective-permute-start(f32[4,384]{1,0:T(4,128)S(1)} %get-tuple-element.32), channel_id=1, source_target_pairs={{1,0},{2,1},{3,2},{4,3},{5,4},{6,5},{7,6},{8,7},{9,8},{10,9},{11,1... | collective-permute-start | bytes 18440 | tf_op jit(solution)/shard_map/ppermute | solution.py:29
  17.6 0.9 %fusion.4 = f32[128]{0:T(128)S(1)} fusion(s32[128]{0:T(128)} %bitcast.41), kind=kOutput, calls=%fused_computation.11 | convolution fusion | flops 548736 | bytes 1024 | tf_op jit(solution)/shard_map/dot_general | solution.py:129
  18.5 0.7 fusion.37
  19.2 0.4 all-to-all-done
  19.6 0.1 mul.110
  19.7 0.3 fusion.9
  20.0 4.4 %collective-permute-start.3 = (f32[4,128]{1,0:T(4,128)S(1)}, f32[4,128]{1,0:T(4,128)S(1)}, u32[]{:S(2)}, u32[]{:S(2)}) collective-permute-start(f32[4,128]{1,0:T(4,128)S(1)} %get-tuple-element.52), channel_id=1, source_target_pairs={{1,0},{2,1},{3,2},{4,3},{5,4},{6,5},{7,6},{8,7},{9,8},{10,9},{11,1... | collective-permute-start | bytes 6152 | tf_op jit(solution)/shard_map/ppermute | solution.py:29
  24.5 2.0 %broadcast_multiply_fusion = bf16[40,256,128]{2,1,0:T(8,128)(2,1)S(1)} fusion(bf16[40,256,128]{2,1,0:T(8,128)(2,1)} %param.18, bf16[256]{0:T(256)(128)(2,1)S(1)} %convert_element_type.46), kind=kLoop, calls=%fused_computation.9 | loop fusion | flops 1310720 | bytes 5243392 | tf_op jit(solution)/shard_map/mul | solution.py:154
  26.5 0.2 broadcast_multiply_fusion.1
  26.7 0.3 pad.46
  27.0 2.7 %copy.14 = bf16[4,8,256,128]{3,1,2,0:T(8,128)(2,1)} copy(bf16[4,8,256,128]{3,2,1,0:T(8,128)(2,1)S(1)} %bitcast.35) | data formatting | bytes 4194304
  29.7 3.2 %copy.16 = bf16[5,8,256,128]{3,1,2,0:T(8,128)(2,1)} copy(bf16[5,8,256,128]{3,2,1,0:T(8,128)(2,1)S(1)} %bitcast.34) | data formatting | bytes 5242880
  32.9 0.1 fusion.45
  33.0 0.1 slice_add_fusion.1
  33.2 0.1 fusion.55
  33.3 0.1 fusion.41
  33.4 0.1 fusion.52
  33.5 0.1 fusion.39
  33.6 0.1 fusion.47
  33.7 0.1 fusion.33
  33.8 0.6 slice_add_fusion
  34.5 1.0 %fusion.8 = f32[256,128]{1,0:T(8,128)} fusion(f32[128,128]{1,0:T(8,128)S(1)} %get-tuple-element.19, s32[128]{0:T(128)S(1)} %fusion.37), kind=kOutput, calls=%fused_computation.21 | convolution fusion | flops 50364416 | bytes 197120 | tf_op jit(solution)/shard_map/dot_general | solution.py:182
  35.5 3.5 %all-to-all-start.1 = ((f32[16,16,128]{2,1,0:T(8,128)}), f32[16,16,128]{2,1,0:T(8,128)S(1)}, u32[]{:S(2)}, u32[]{:S(2)}) async-start(f32[16,16,128]{2,1,0:T(8,128)} %bitcast.5), calls=%async_computation.1 | async-start | bytes 262144 | tf_op jit(solution)/shard_map/all_to_all | solution.py:183
  39.0 5.3 %fusion = f32[70,70]{1,0:T(8,128)S(1)} fusion(bf16[30,32768]{1,0:T(8,128)(2,1)} %bitcast.37, bf16[40,32768]{1,0:T(8,128)(2,1)} %bitcast.36), kind=kOutput, calls=%fused_computation.2 | convolution fusion | flops 330301440 | bytes 4607120 | tf_op jit(solution)/shard_map/dot_general | solution.py:159
  44.3 2.5 %all-to-all-done.1 = f32[16,16,128]{2,1,0:T(8,128)S(1)} async-done(((f32[16,16,128]{2,1,0:T(8,128)}), f32[16,16,128]{2,1,0:T(8,128)S(1)}, u32[]{:S(2)}, u32[]{:S(2)}) %all-to-all-start.1) | async-done | bytes 131104 | tf_op jit(solution)/shard_map/all_to_all | solution.py:183
  46.9 0.1 fusion.6
  47.0 2.2 %multiply_reduce_fusion.3 = f32[30]{0:T(128)S(1)} fusion(bf16[30,256,128]{2,1,0:T(8,128)(2,1)} %param.20, f32[256,128]{1,0:T(8,128)S(1)} %fusion.6), kind=kLoop, calls=%fused_computation.7 | loop fusion | flops 2949090 | bytes 2097272 | tf_op jit(solution)/shard_map/reduce_sum | solution.py:188
  49.2 0.8 %multiply_reduce_fusion.1 = f32[40]{0:T(128)S(1)} fusion(bf16[40,256,128]{2,1,0:T(8,128)(2,1)S(1)} %copy-done, f32[256,128]{1,0:T(8,128)S(1)} %fusion.6), kind=kLoop, calls=%fused_computation.1 | loop fusion | flops 3932120 | bytes 2752672 | tf_op jit(solution)/shard_map/reduce_sum | solution.py:187
  50.2 1.2 %collective-permute-done.4 = f32[71,70]{1,0:T(8,128)S(1)} collective-permute-done((f32[71,70]{1,0:T(8,128)S(1)}, f32[71,70]{1,0:T(8,128)S(1)}, u32[]{:S(2)}, u32[]{:S(2)}) %collective-permute-start.4) | collective-permute-done | bytes 19912 | tf_op jit(solution)/shard_map/ppermute | solution.py:21
  51.5 3.9 %collective-permute-done.5 = f32[71,70]{1,0:T(8,128)S(1)} collective-permute-done((f32[71,70]{1,0:T(8,128)S(1)}, f32[71,70]{1,0:T(8,128)S(1)}, u32[]{:S(2)}, u32[]{:S(2)}) %collective-permute-start.5) | collective-permute-done | bytes 19912 | tf_op jit(solution)/shard_map/ppermute | solution.py:21
  55.5 3.9 %collective-permute-done.6 = f32[71,70]{1,0:T(8,128)S(1)} collective-permute-done((f32[71,70]{1,0:T(8,128)S(1)}, f32[71,70]{1,0:T(8,128)S(1)}, u32[]{:S(2)}, u32[]{:S(2)}) %collective-permute-start.6) | collective-permute-done | bytes 19912 | tf_op jit(solution)/shard_map/ppermute | solution.py:21
  59.4 0.3 collective-permute-start.7
  59.7 4.5 %collective-permute-done.7 = f32[71,70]{1,0:T(8,128)S(1)} collective-permute-done((f32[71,70]{1,0:T(8,128)S(1)}, f32[71,70]{1,0:T(8,128)S(1)}, u32[]{:S(2)}, u32[]{:S(2)}) %collective-permute-start.7) | collective-permute-done | bytes 19912 | tf_op jit(solution)/shard_map/ppermute | solution.py:21
  64.3 0.6 add.137.sums_ref
  64.9 6.3 %shard_map.121 = (f32[1,40]{1,0:T(1,128)}, f32[1,30]{1,0:T(1,128)}) custom-call(f32[71,70]{1,0:T(8,128)} %add.137.sums_ref), custom_call_target="tpu_custom_call" | custom-call | tf_op jit(solution)/shard_map/pallas_call | solution.py:102
  71.2 0.6 reduce-precision_bitcast_fusion.1
  71.8 0.7 reduce-precision_bitcast_fusion
  72.4 2.0 %multiply_reduce_fusion.2 = f32[256,128]{1,0:T(8,128)S(1)} fusion(bf16[30,256,128]{2,1,0:T(8,128)(2,1)} %param.21, f32[30]{0:T(128)S(1)} %reduce-precision_bitcast_fusion), kind=kLoop, calls=%fused_computation.6 | loop fusion | flops 2916352 | bytes 2097272 | tf_op jit(solution)/shard_map/reduce_sum | solution.py:196
  74.5 0.8 %multiply_reduce_fusion = f32[256,128]{1,0:T(8,128)S(1)} fusion(bf16[40,256,128]{2,1,0:T(8,128)(2,1)S(1)} %copy-done.2, f32[40]{0:T(128)S(1)} %reduce-precision_bitcast_fusion.1), kind=kLoop, calls=%fused_computation | loop fusion | flops 3899392 | bytes 2752672 | tf_op jit(solution)/shard_map/reduce_sum | solution.py:195
  75.2 0.8 %fusion.7 = f32[256,128]{1,0:T(8,128)} fusion(f32[16,16,128]{2,1,0:T(8,128)S(1)} %all-to-all-done.1, f32[256,128]{1,0:T(8,128)S(1)} %multiply_reduce_fusion, f32[256,128]{1,0:T(8,128)S(1)} %multiply_reduce_fusion.2, f32[256]{0:T(256)S(1)} %mul.110), kind=kLoop, calls=%fused_computation.19 | loop fusion | flops 98304 | bytes 525312 | tf_op jit(solution)/shard_map/mul | solution.py:198
  (45 shorter events, 0.5 us)
Async XLA Ops:
  3.1 16.4 %all-to-all-start = ((f32[16,24,128]{2,1,0:T(8,128)}), f32[16,24,128]{2,1,0:T(8,128)S(1)}, u32[]{:S(2)}, u32[]{:S(2)}) async-start(f32[16,24,128]{2,1,0:T(8,128)} %pad_maximum_fusion), calls=%async_computation | async-start | bytes 393216 | tf_op jit(solution)/shard_map/all_to_all | solution.py:147
  13.1 6.1 %collective-permute-start = (f32[4,384]{1,0:T(4,128)S(1)}, f32[4,384]{1,0:T(4,128)S(1)}, u32[]{:S(2)}, u32[]{:S(2)}) collective-permute-start(f32[4,384]{1,0:T(4,128)S(1)} %get-tuple-element.31), channel_id=1, source_target_pairs={{0,1},{1,2},{2,3},{3,4},{4,5},{5,6},{6,7},{7,8},{8,9},{9,10},{10,1... | collective-permute-start | bytes 18440 | tf_op jit(solution)/shard_map/ppermute | solution.py:28
  13.5 5.6 %collective-permute-start.2 = (f32[4,384]{1,0:T(4,128)S(1)}, f32[4,384]{1,0:T(4,128)S(1)}, u32[]{:S(2)}, u32[]{:S(2)}) collective-permute-start(f32[4,384]{1,0:T(4,128)S(1)} %get-tuple-element.32), channel_id=1, source_target_pairs={{1,0},{2,1},{3,2},{4,3},{5,4},{6,5},{7,6},{8,7},{9,8},{10,9},{11,1... | collective-permute-start | bytes 18440 | tf_op jit(solution)/shard_map/ppermute | solution.py:29
  20.0 12.9 %collective-permute-start.1 = (f32[4,128]{1,0:T(4,128)S(1)}, f32[4,128]{1,0:T(4,128)S(1)}, u32[]{:S(2)}, u32[]{:S(2)}) collective-permute-start(f32[4,128]{1,0:T(4,128)S(1)} %get-tuple-element.51), channel_id=1, source_target_pairs={{0,1},{1,2},{2,3},{3,4},{4,5},{5,6},{6,7},{7,8},{8,9},{9,10},{10,1... | collective-permute-start | bytes 6152 | tf_op jit(solution)/shard_map/ppermute | solution.py:28
  20.0 6.4 %copy-start.1 = (bf16[30,256,128]{2,1,0:T(8,128)(2,1)S(1)}, bf16[30,256,128]{2,1,0:T(8,128)(2,1)}, u32[]{:S(2)}) copy-start(bf16[30,256,128]{2,1,0:T(8,128)(2,1)} %param.20) | copy-start | bytes 5898244
  20.0 12.8 %collective-permute-start.3 = (f32[4,128]{1,0:T(4,128)S(1)}, f32[4,128]{1,0:T(4,128)S(1)}, u32[]{:S(2)}, u32[]{:S(2)}) collective-permute-start(f32[4,128]{1,0:T(4,128)S(1)} %get-tuple-element.52), channel_id=1, source_target_pairs={{1,0},{2,1},{3,2},{4,3},{5,4},{6,5},{7,6},{8,7},{9,8},{10,9},{11,1... | collective-permute-start | bytes 6152 | tf_op jit(solution)/shard_map/ppermute | solution.py:29
  29.7 3.2 %copy-start.3 = (f32[128,128]{1,0:T(8,128)S(1)}, f32[128,128]{1,0:T(8,128)}, u32[]{:S(2)}) copy-start(f32[128,128]{1,0:T(8,128)} %param.14) | copy-start | bytes 196612
  29.7 3.2 %copy-start.4 = (f32[128,128]{1,0:T(8,128)S(1)}, f32[128,128]{1,0:T(8,128)}, u32[]{:S(2)}) copy-start(f32[128,128]{1,0:T(8,128)} %param.15) | copy-start | bytes 196612
  29.7 3.2 %copy-start.5 = (f32[128,128]{1,0:T(8,128)S(1)}, f32[128,128]{1,0:T(8,128)}, u32[]{:S(2)}) copy-start(f32[128,128]{1,0:T(8,128)} %param.16) | copy-start | bytes 196612
  34.5 9.9 %copy-start.6 = (f32[128,128]{1,0:T(8,128)}, f32[128,128]{1,0:T(8,128)S(1)}, u32[]{:S(2)}) copy-start(f32[128,128]{1,0:T(8,128)S(1)} %get-tuple-element.19) | copy-start | bytes 196612
  35.5 11.4 %all-to-all-start.1 = ((f32[16,16,128]{2,1,0:T(8,128)}), f32[16,16,128]{2,1,0:T(8,128)S(1)}, u32[]{:S(2)}, u32[]{:S(2)}) async-start(f32[16,16,128]{2,1,0:T(8,128)} %bitcast.5), calls=%async_computation.1 | async-start | bytes 262144 | tf_op jit(solution)/shard_map/all_to_all | solution.py:183
  39.0 7.9 %copy-start.7 = (f32[256,128]{1,0:T(8,128)S(1)}, f32[256,128]{1,0:T(8,128)}, u32[]{:S(2)}) copy-start(f32[256,128]{1,0:T(8,128)} %param.13) | copy-start | bytes 393220
  39.0 10.2 %copy-start = (bf16[40,256,128]{2,1,0:T(8,128)(2,1)S(1)}, bf16[40,256,128]{2,1,0:T(8,128)(2,1)}, u32[]{:S(2)}) copy-start(bf16[40,256,128]{2,1,0:T(8,128)(2,1)} %param.18) | copy-start | bytes 7864324
  50.0 24.4 %copy-start.2 = (bf16[40,256,128]{2,1,0:T(8,128)(2,1)S(1)}, bf16[40,256,128]{2,1,0:T(8,128)(2,1)}, u32[]{:S(2)}) copy-start(bf16[40,256,128]{2,1,0:T(8,128)(2,1)} %param.19) | copy-start | bytes 7864324
  50.1 1.3 %collective-permute-start.4 = (f32[71,70]{1,0:T(8,128)S(1)}, f32[71,70]{1,0:T(8,128)S(1)}, u32[]{:S(2)}, u32[]{:S(2)}) collective-permute-start(f32[71,70]{1,0:T(8,128)S(1)} %pad_maximum_fusion.1), channel_id=1, source_target_pairs={{0,1},{1,0},{2,3},{3,2},{4,5},{5,4},{6,7},{7,6},{8,9},{9,8},{10,11... | collective-permute-start | bytes 59648 | tf_op jit(solution)/shard_map/ppermute | solution.py:21
  51.4 4.0 %collective-permute-start.5 = (f32[71,70]{1,0:T(8,128)S(1)}, f32[71,70]{1,0:T(8,128)S(1)}, u32[]{:S(2)}, u32[]{:S(2)}) collective-permute-start(f32[71,70]{1,0:T(8,128)S(1)} %fusion.59), channel_id=1, source_target_pairs={{0,2},{1,3},{2,0},{3,1},{4,6},{5,7},{6,4},{7,5},{8,10},{9,11},{10,... | collective-permute-start | bytes 59648 | tf_op jit(solution)/shard_map/ppermute | solution.py:21
  55.5 4.0 %collective-permute-start.6 = (f32[71,70]{1,0:T(8,128)S(1)}, f32[71,70]{1,0:T(8,128)S(1)}, u32[]{:S(2)}, u32[]{:S(2)}) collective-permute-start(f32[71,70]{1,0:T(8,128)S(1)} %add.135), channel_id=1, source_target_pairs={{0,4},{1,5},{2,6},{3,7},{4,0},{5,1},{6,2},{7,3},{8,12},{9,13},{10,... | collective-permute-start | bytes 59648 | tf_op jit(solution)/shard_map/ppermute | solution.py:21
  59.4 4.9 %collective-permute-start.7 = (f32[71,70]{1,0:T(8,128)S(1)}, f32[71,70]{1,0:T(8,128)S(1)}, u32[]{:S(2)}, u32[]{:S(2)}) collective-permute-start(f32[71,70]{1,0:T(8,128)S(1)} %add.136), channel_id=1, source_target_pairs={{0,8},{1,9},{2,10},{3,11},{4,12},{5,13},{6,14},{7,15},{8,0},{9,1},... | collective-permute-start | bytes 59648 | tf_op jit(solution)/shard_map/ppermute | solution.py:21

commit v2 on v1

--- a/solution.py
+++ b/solution.py
@@ -140,8 +140,7 @@
     edge = jnp.concatenate([displace, velocity, stiffness], axis=1)
     edge_below, edge_above = halo_pair(edge, width, "tile")
 
-    flag_count = 8 - per_pair % 8
-    flag_rows = jnp.zeros((tile_count, flag_count, lanes), jnp.float32)
+    flag_rows = jnp.zeros((tile_count, 1, lanes), jnp.float32)
     flag_rows = flag_rows.at[:, 0, :per_pair].set(flags)
     sent = jnp.concatenate([fluid_press.reshape(tile_count, per_pair, lanes), flag_rows], axis=1)
     got = lax.all_to_all(sent, "tile", split_axis=0, concat_axis=0, tiled=True)
@@ -160,18 +159,14 @@
 
     pressure = jnp.dot(chooser, returned, precision=high)
     press_below, press_above = halo_pair(pressure, width, "tile")
-    packed = jnp.concatenate(
-        [
-            jnp.concatenate([edge_below, press_below], axis=1),
-            jnp.concatenate([edge, pressure], axis=1),
-            jnp.concatenate([edge_above, press_above], axis=1),
-        ],
-        axis=0,
-    )
-    field = packed[:, :lanes]
-    speed = packed[:, lanes : 2 * lanes]
-    stiff = packed[:, 2 * lanes : 3 * lanes]
-    press = packed[:, 3 * lanes :]
+    def extended(middle, which):
+        cut = slice(which * lanes, (which + 1) * lanes)
+        return jnp.concatenate([edge_below[:, cut], middle, edge_above[:, cut]], axis=0)
+
+    field = extended(displace, 0)
+    speed = extended(velocity, 1)
+    stiff = extended(stiffness, 2)
+    press = jnp.concatenate([press_below, pressure, press_above], axis=0)
     for _ in range(SUBSTEPS):
         lapl = jnp.roll(field, 1, 0) + jnp.roll(field, -1, 0) + sides(field) - 4.0 * field
         speed = speed + step_dt * (stiff * lapl + press - damping * speed)

time: 76.6 us -> 77.1 us (level)
  other arithmetic: 15.1 us -> 16 us
    concatenate x1, other arithmetic: 0.03 us -> 0.85 us  [extended(): jnp.concatenate([edge_below[:, cut], middle, edge_above[:, cut]], axis=0)]
  transfers between devices with their start and end apart: 10 -> 10, of which waited for: 6 -> 5; matrix products, arithmetic and copies ran while one was open for 23% -> 24% of each run, Pallas kernels for 0% -> 0%
where the time goes in v2:
time: 77.1 us; the launch traced here: 76.4 us
  starting transfers between devices  20.4 us (26%)
  waiting for transfers between devices  16.2 us (21%)
  other arithmetic  16 us (21%)
  local copies, waits for them, and re-layouts  9.28 us (12%)
  matrix products  7.43 us (10%)
  Pallas kernels  6.21 us (8%)
  between operations  0.96 us (1%)
    ppermute x4, waiting for transfers between devices, tree_sum(): lax.ppermute(value, axis, [(i, i ^ stride) for i in range(count)])  13.6 us
    ppermute x2, starting transfers between devices, halo_pair(): lax.ppermute(cells[:width], axis, [((i + 1) % count, i) for i in range(co...  8.46 us
    unnamed x21, local copies, waits for them, and re-layouts  7.9 us
    all_to_all x1, starting transfers between devices, body(): got = lax.all_to_all(sent, 'tile', split_axis=0, concat_axis=0, tiled=True)  7.41 us
    pallas_call x1, Pallas kernels, solve_both(): coeff, past = pl.pallas_call(solve_kernel, out_shape=shapes)(sums)  6.21 us
    dot_general x1, matrix products, body(): lax.dot_general(cols, cols, (((1,), (1,)), ((), ())), preferred_element_t...  5.29 us
    all_to_all x1, starting transfers between devices, body(): lax.all_to_all(outgoing, 'tile', split_axis=0, concat_axis=0, tiled=True)  3.51 us
    all_to_all x1, waiting for transfers between devices, body(): lax.all_to_all(outgoing, 'tile', split_axis=0, concat_axis=0, tiled=True)  2.54 us
  transfers between devices with their start and end apart: 10, of which 5 were waited for; matrix products, arithmetic and copies ran while one was open for 24% of the time, Pallas kernels for 0%

profile of v2, /device:TPU:0, one launch (start us, length us, event | category | flops | bytes accessed | tf_op | source)
XLA Modules:
  0.0 76.4 jit_solution(13588920896067929489)
XLA Ops:
  0.6 0.8 %convert_reduce_fusion = f32[16]{0:T(128)S(1)} fusion(s32[128]{0:T(128)} %bitcast.40), kind=kLoop, calls=%fused_computation.64 | loop fusion | flops 6128 | bytes 576 | tf_op jit(solution)/shard_map/reduce_sum | solution.py:135
  1.4 0.1 iota_compare_fusion.7
  1.5 1.6 %pad_maximum_fusion = f32[16,17,128]{2,1,0:T(8,128)} fusion(f32[16,1,128]{2,1,0:T(1,128)S(1)} %pad_convert_fusion, f32[16,16,128]{2,1,0:T(8,128)} %bitcast.39), kind=kLoop, calls=%fused_computation.13 | loop fusion | flops 34816 | bytes 278528 | tf_op jit(solution)/shard_map/concatenate | solution.py:145
  3.1 7.4 %all-to-all-start = ((f32[16,17,128]{2,1,0:T(8,128)}), f32[16,17,128]{2,1,0:T(8,128)S(1)}, u32[]{:S(2)}, u32[]{:S(2)}) async-start(f32[16,17,128]{2,1,0:T(8,128)} %pad_maximum_fusion), calls=%async_computation | async-start | bytes 393216 | tf_op jit(solution)/shard_map/all_to_all | solution.py:146
  10.5 0.8 %constant_dynamic-update-slice_fusion.2 = f32[128,384]{1,0:T(8,128)S(1)} fusion(f32[128,128]{1,0:T(8,128)} %param.14), kind=kLoop, calls=%fused_computation.63 | loop fusion | bytes 131072
  11.4 0.8 %constant_dynamic-update-slice_fusion.1 = f32[128,384]{1,0:T(8,128)S(1)} fusion(f32[128,384]{1,0:T(8,128)S(1)} %constant_dynamic-update-slice_fusion.2, f32[128,128]{1,0:T(8,128)} %param.15), kind=kLoop, calls=%fused_computation.62 | loop fusion | bytes 131072
  12.2 0.8 %constant_dynamic-update-slice_fusion = f32[128,384]{1,0:T(8,128)S(1)} fusion(f32[128,384]{1,0:T(8,128)S(1)} %constant_dynamic-update-slice_fusion.1, f32[128,128]{1,0:T(8,128)} %param.16), kind=kLoop, calls=%fused_computation.61 | loop fusion | bytes 131072 | tf_op jit(solution)/shard_map/concatenate | solution.py:140
  13.1 0.5 collective-permute-start
  13.5 4.0 %collective-permute-start.1 = (f32[4,384]{1,0:T(4,128)S(1)}, f32[4,384]{1,0:T(4,128)S(1)}, u32[]{:S(2)}, u32[]{:S(2)}) collective-permute-start(f32[4,384]{1,0:T(4,128)S(1)} %get-tuple-element.28), channel_id=1, source_target_pairs={{1,0},{2,1},{3,2},{4,3},{5,4},{6,5},{7,6},{8,7},{9,8},{10,9},{11,1... | collective-permute-start | bytes 18440 | tf_op jit(solution)/shard_map/ppermute | solution.py:29
  17.6 0.9 %fusion.4 = f32[128]{0:T(128)S(1)} fusion(s32[128]{0:T(128)} %bitcast.41), kind=kOutput, calls=%fused_computation.11 | convolution fusion | flops 548736 | bytes 1024 | tf_op jit(solution)/shard_map/dot_general | solution.py:129
  18.5 0.7 fusion.37
  19.2 0.9 %pad_maximum_fusion.1 = f32[136,128]{1,0:T(8,128)S(1)} fusion(f32[4,128]{1,0:T(4,128)S(1)} %get-tuple-element.58, f32[128,128]{1,0:T(8,128)} %param.14, f32[4,128]{1,0:T(4,128)S(1)} %get-tuple-element.55), kind=kLoop, calls=%fused_computation.22 | loop fusion | flops 34816 | bytes 139264 | tf_op jit(solution)/shard_map/concatenate | solution.py:164
  20.0 0.1 fusion.56
  20.2 0.1 mul.110
  20.3 0.3 fusion.9
  20.6 4.4 %collective-permute-start.3 = (f32[4,128]{1,0:T(4,128)S(1)}, f32[4,128]{1,0:T(4,128)S(1)}, u32[]{:S(2)}, u32[]{:S(2)}) collective-permute-start(f32[4,128]{1,0:T(4,128)S(1)} %get-tuple-element.52), channel_id=1, source_target_pairs={{1,0},{2,1},{3,2},{4,3},{5,4},{6,5},{7,6},{8,7},{9,8},{10,9},{11,1... | collective-permute-start | bytes 6152 | tf_op jit(solution)/shard_map/ppermute | solution.py:29
  25.1 2.0 %broadcast_multiply_fusion = bf16[40,256,128]{2,1,0:T(8,128)(2,1)S(1)} fusion(bf16[40,256,128]{2,1,0:T(8,128)(2,1)} %param.18, bf16[256]{0:T(256)(128)(2,1)S(1)} %convert_element_type.46), kind=kLoop, calls=%fused_computation.9 | loop fusion | flops 1310720 | bytes 5243392 | tf_op jit(solution)/shard_map/mul | solution.py:153
  27.1 0.2 broadcast_multiply_fusion.1
  27.3 0.3 pad.50
  27.6 2.7 %copy.14 = bf16[4,8,256,128]{3,1,2,0:T(8,128)(2,1)} copy(bf16[4,8,256,128]{3,2,1,0:T(8,128)(2,1)S(1)} %bitcast.35) | data formatting | bytes 4194304
  30.3 3.2 %copy.16 = bf16[5,8,256,128]{3,1,2,0:T(8,128)(2,1)} copy(bf16[5,8,256,128]{3,2,1,0:T(8,128)(2,1)S(1)} %bitcast.34) | data formatting | bytes 5242880
  33.5 0.1 fusion.39
  33.6 0.1 fusion.54
  33.7 0.1 fusion.42
  33.9 0.1 fusion.51
  34.0 0.1 fusion.40
  34.1 0.1 fusion.46
  34.2 0.1 fusion.33
  34.3 0.6 slice_add_fusion
  35.0 1.0 %fusion.8 = f32[256,128]{1,0:T(8,128)} fusion(f32[128,128]{1,0:T(8,128)S(1)} %get-tuple-element.19, s32[128]{0:T(128)S(1)} %fusion.37), kind=kOutput, calls=%fused_computation.20 | convolution fusion | flops 50364416 | bytes 197120 | tf_op jit(solution)/shard_map/dot_general | solution.py:177
  36.0 3.5 %all-to-all-start.1 = ((f32[16,16,128]{2,1,0:T(8,128)}), f32[16,16,128]{2,1,0:T(8,128)S(1)}, u32[]{:S(2)}, u32[]{:S(2)}) async-start(f32[16,16,128]{2,1,0:T(8,128)} %bitcast.5), calls=%async_computation.1 | async-start | bytes 262144 | tf_op jit(solution)/shard_map/all_to_all | solution.py:178
  39.5 5.3 %fusion = f32[70,70]{1,0:T(8,128)S(1)} fusion(bf16[30,32768]{1,0:T(8,128)(2,1)} %bitcast.37, bf16[40,32768]{1,0:T(8,128)(2,1)} %bitcast.36), kind=kOutput, calls=%fused_computation.2 | convolution fusion | flops 330301440 | bytes 4607120 | tf_op jit(solution)/shard_map/dot_general | solution.py:158
  44.8 2.5 %all-to-all-done.1 = f32[16,16,128]{2,1,0:T(8,128)S(1)} async-done(((f32[16,16,128]{2,1,0:T(8,128)}), f32[16,16,128]{2,1,0:T(8,128)S(1)}, u32[]{:S(2)}, u32[]{:S(2)}) %all-to-all-start.1) | async-done | bytes 131104 | tf_op jit(solution)/shard_map/all_to_all | solution.py:178
  47.4 0.1 fusion.6
  47.5 2.2 %multiply_reduce_fusion.3 = f32[30]{0:T(128)S(1)} fusion(bf16[30,256,128]{2,1,0:T(8,128)(2,1)} %param.20, f32[256,128]{1,0:T(8,128)S(1)} %fusion.6), kind=kLoop, calls=%fused_computation.7 | loop fusion | flops 2949090 | bytes 2097272 | tf_op jit(solution)/shard_map/reduce_sum | solution.py:183
  49.7 0.8 %multiply_reduce_fusion.1 = f32[40]{0:T(128)S(1)} fusion(bf16[40,256,128]{2,1,0:T(8,128)(2,1)S(1)} %copy-done, f32[256,128]{1,0:T(8,128)S(1)} %fusion.6), kind=kLoop, calls=%fused_computation.1 | loop fusion | flops 3932120 | bytes 2752672 | tf_op jit(solution)/shard_map/reduce_sum | solution.py:182
  50.7 1.2 %collective-permute-done.4 = f32[71,70]{1,0:T(8,128)S(1)} collective-permute-done((f32[71,70]{1,0:T(8,128)S(1)}, f32[71,70]{1,0:T(8,128)S(1)}, u32[]{:S(2)}, u32[]{:S(2)}) %collective-permute-start.4) | collective-permute-done | bytes 19912 | tf_op jit(solution)/shard_map/ppermute | solution.py:21
  52.0 3.9 %collective-permute-done.5 = f32[71,70]{1,0:T(8,128)S(1)} collective-permute-done((f32[71,70]{1,0:T(8,128)S(1)}, f32[71,70]{1,0:T(8,128)S(1)}, u32[]{:S(2)}, u32[]{:S(2)}) %collective-permute-start.5) | collective-permute-done | bytes 19912 | tf_op jit(solution)/shard_map/ppermute | solution.py:21
  55.9 3.9 %collective-permute-done.6 = f32[71,70]{1,0:T(8,128)S(1)} collective-permute-done((f32[71,70]{1,0:T(8,128)S(1)}, f32[71,70]{1,0:T(8,128)S(1)}, u32[]{:S(2)}, u32[]{:S(2)}) %collective-permute-start.6) | collective-permute-done | bytes 19912 | tf_op jit(solution)/shard_map/ppermute | solution.py:21
  59.9 0.3 collective-permute-start.7
  60.2 4.5 %collective-permute-done.7 = f32[71,70]{1,0:T(8,128)S(1)} collective-permute-done((f32[71,70]{1,0:T(8,128)S(1)}, f32[71,70]{1,0:T(8,128)S(1)}, u32[]{:S(2)}, u32[]{:S(2)}) %collective-permute-start.7) | collective-permute-done | bytes 19912 | tf_op jit(solution)/shard_map/ppermute | solution.py:21
  64.7 0.6 add.137.sums_ref
  65.4 6.2 %shard_map.121 = (f32[1,40]{1,0:T(1,128)}, f32[1,30]{1,0:T(1,128)}) custom-call(f32[71,70]{1,0:T(8,128)} %add.137.sums_ref), custom_call_target="tpu_custom_call" | custom-call | tf_op jit(solution)/shard_map/pallas_call | solution.py:102
  71.6 0.7 reduce-precision_bitcast_fusion.1
  72.3 0.6 reduce-precision_bitcast_fusion
  72.9 2.0 %multiply_reduce_fusion.2 = f32[256,128]{1,0:T(8,128)S(1)} fusion(bf16[30,256,128]{2,1,0:T(8,128)(2,1)} %param.21, f32[30]{0:T(128)S(1)} %reduce-precision_bitcast_fusion), kind=kLoop, calls=%fused_computation.6 | loop fusion | flops 2916352 | bytes 2097272 | tf_op jit(solution)/shard_map/reduce_sum | solution.py:191
  74.9 0.8 multiply_reduce_fusion
  75.6 0.8 %fusion.7 = f32[256,128]{1,0:T(8,128)} fusion(f32[16,16,128]{2,1,0:T(8,128)S(1)} %all-to-all-done.1, f32[256,128]{1,0:T(8,128)S(1)} %multiply_reduce_fusion, f32[256,128]{1,0:T(8,128)S(1)} %multiply_reduce_fusion.2, f32[256]{0:T(256)S(1)} %mul.110), kind=kLoop, calls=%fused_computation.18 | loop fusion | flops 98304 | bytes 525312 | tf_op jit(solution)/shard_map/mul | solution.py:193
  (47 shorter events, 0.5 us)
Async XLA Ops:
  3.1 17.0 %all-to-all-start = ((f32[16,17,128]{2,1,0:T(8,128)}), f32[16,17,128]{2,1,0:T(8,128)S(1)}, u32[]{:S(2)}, u32[]{:S(2)}) async-start(f32[16,17,128]{2,1,0:T(8,128)} %pad_maximum_fusion), calls=%async_computation | async-start | bytes 393216 | tf_op jit(solution)/shard_map/all_to_all | solution.py:146
  13.1 6.1 %collective-permute-start = (f32[4,384]{1,0:T(4,128)S(1)}, f32[4,384]{1,0:T(4,128)S(1)}, u32[]{:S(2)}, u32[]{:S(2)}) collective-permute-start(f32[4,384]{1,0:T(4,128)S(1)} %get-tuple-element.27), channel_id=1, source_target_pairs={{0,1},{1,2},{2,3},{3,4},{4,5},{5,6},{6,7},{7,8},{8,9},{9,10},{10,1... | collective-permute-start | bytes 18440 | tf_op jit(solution)/shard_map/ppermute | solution.py:28
  13.5 5.6 %collective-permute-start.1 = (f32[4,384]{1,0:T(4,128)S(1)}, f32[4,384]{1,0:T(4,128)S(1)}, u32[]{:S(2)}, u32[]{:S(2)}) collective-permute-start(f32[4,384]{1,0:T(4,128)S(1)} %get-tuple-element.28), channel_id=1, source_target_pairs={{1,0},{2,1},{3,2},{4,3},{5,4},{6,5},{7,6},{8,7},{9,8},{10,9},{11,1... | collective-permute-start | bytes 18440 | tf_op jit(solution)/shard_map/ppermute | solution.py:29
  20.6 12.9 %collective-permute-start.2 = (f32[4,128]{1,0:T(4,128)S(1)}, f32[4,128]{1,0:T(4,128)S(1)}, u32[]{:S(2)}, u32[]{:S(2)}) collective-permute-start(f32[4,128]{1,0:T(4,128)S(1)} %get-tuple-element.51), channel_id=1, source_target_pairs={{0,1},{1,2},{2,3},{3,4},{4,5},{5,6},{6,7},{7,8},{8,9},{9,10},{10,1... | collective-permute-start | bytes 6152 | tf_op jit(solution)/shard_map/ppermute | solution.py:28
  20.6 6.4 %copy-start.1 = (bf16[30,256,128]{2,1,0:T(8,128)(2,1)S(1)}, bf16[30,256,128]{2,1,0:T(8,128)(2,1)}, u32[]{:S(2)}) copy-start(bf16[30,256,128]{2,1,0:T(8,128)(2,1)} %param.20) | copy-start | bytes 5898244
  20.6 12.8 %collective-permute-start.3 = (f32[4,128]{1,0:T(4,128)S(1)}, f32[4,128]{1,0:T(4,128)S(1)}, u32[]{:S(2)}, u32[]{:S(2)}) collective-permute-start(f32[4,128]{1,0:T(4,128)S(1)} %get-tuple-element.52), channel_id=1, source_target_pairs={{1,0},{2,1},{3,2},{4,3},{5,4},{6,5},{7,6},{8,7},{9,8},{10,9},{11,1... | collective-permute-start | bytes 6152 | tf_op jit(solution)/shard_map/ppermute | solution.py:29
  30.3 3.2 %copy-start.3 = (f32[128,128]{1,0:T(8,128)S(1)}, f32[128,128]{1,0:T(8,128)}, u32[]{:S(2)}) copy-start(f32[128,128]{1,0:T(8,128)} %param.16) | copy-start | bytes 196612
  30.3 3.2 %copy-start.4 = (f32[128,128]{1,0:T(8,128)S(1)}, f32[128,128]{1,0:T(8,128)}, u32[]{:S(2)}) copy-start(f32[128,128]{1,0:T(8,128)} %param.14) | copy-start | bytes 196612
  30.3 3.2 %copy-start.6 = (f32[128,128]{1,0:T(8,128)S(1)}, f32[128,128]{1,0:T(8,128)}, u32[]{:S(2)}) copy-start(f32[128,128]{1,0:T(8,128)} %param.15) | copy-start | bytes 196612
  35.0 9.9 %copy-start.5 = (f32[128,128]{1,0:T(8,128)}, f32[128,128]{1,0:T(8,128)S(1)}, u32[]{:S(2)}) copy-start(f32[128,128]{1,0:T(8,128)S(1)} %get-tuple-element.19) | copy-start | bytes 196612
  36.0 11.4 %all-to-all-start.1 = ((f32[16,16,128]{2,1,0:T(8,128)}), f32[16,16,128]{2,1,0:T(8,128)S(1)}, u32[]{:S(2)}, u32[]{:S(2)}) async-start(f32[16,16,128]{2,1,0:T(8,128)} %bitcast.5), calls=%async_computation.1 | async-start | bytes 262144 | tf_op jit(solution)/shard_map/all_to_all | solution.py:178
  39.5 7.9 %copy-start.7 = (f32[256,128]{1,0:T(8,128)S(1)}, f32[256,128]{1,0:T(8,128)}, u32[]{:S(2)}) copy-start(f32[256,128]{1,0:T(8,128)} %param.13) | copy-start | bytes 393220
  39.5 10.2 %copy-start = (bf16[40,256,128]{2,1,0:T(8,128)(2,1)S(1)}, bf16[40,256,128]{2,1,0:T(8,128)(2,1)}, u32[]{:S(2)}) copy-start(bf16[40,256,128]{2,1,0:T(8,128)(2,1)} %param.18) | copy-start | bytes 7864324
  50.5 24.4 %copy-start.2 = (bf16[40,256,128]{2,1,0:T(8,128)(2,1)S(1)}, bf16[40,256,128]{2,1,0:T(8,128)(2,1)}, u32[]{:S(2)}) copy-start(bf16[40,256,128]{2,1,0:T(8,128)(2,1)} %param.19) | copy-start | bytes 7864324
  50.6 1.3 %collective-permute-start.4 = (f32[71,70]{1,0:T(8,128)S(1)}, f32[71,70]{1,0:T(8,128)S(1)}, u32[]{:S(2)}, u32[]{:S(2)}) collective-permute-start(f32[71,70]{1,0:T(8,128)S(1)} %pad_maximum_fusion.5), channel_id=1, source_target_pairs={{0,1},{1,0},{2,3},{3,2},{4,5},{5,4},{6,7},{7,6},{8,9},{9,8},{10,11... | collective-permute-start | bytes 59648 | tf_op jit(solution)/shard_map/ppermute | solution.py:21
  51.9 4.0 %collective-permute-start.5 = (f32[71,70]{1,0:T(8,128)S(1)}, f32[71,70]{1,0:T(8,128)S(1)}, u32[]{:S(2)}, u32[]{:S(2)}) collective-permute-start(f32[71,70]{1,0:T(8,128)S(1)} %fusion.62), channel_id=1, source_target_pairs={{0,2},{1,3},{2,0},{3,1},{4,6},{5,7},{6,4},{7,5},{8,10},{9,11},{10,... | collective-permute-start | bytes 59648 | tf_op jit(solution)/shard_map/ppermute | solution.py:21
  55.9 4.0 %collective-permute-start.6 = (f32[71,70]{1,0:T(8,128)S(1)}, f32[71,70]{1,0:T(8,128)S(1)}, u32[]{:S(2)}, u32[]{:S(2)}) collective-permute-start(f32[71,70]{1,0:T(8,128)S(1)} %add.135), channel_id=1, source_target_pairs={{0,4},{1,5},{2,6},{3,7},{4,0},{5,1},{6,2},{7,3},{8,12},{9,13},{10,... | collective-permute-start | bytes 59648 | tf_op jit(solution)/shard_map/ppermute | solution.py:21
  59.9 4.9 %collective-permute-start.7 = (f32[71,70]{1,0:T(8,128)S(1)}, f32[71,70]{1,0:T(8,128)S(1)}, u32[]{:S(2)}, u32[]{:S(2)}) collective-permute-start(f32[71,70]{1,0:T(8,128)S(1)} %add.136), channel_id=1, source_target_pairs={{0,8},{1,9},{2,10},{3,11},{4,12},{5,13},{6,14},{7,15},{8,0},{9,1},... | collective-permute-start | bytes 59648 | tf_op jit(solution)/shard_map/ppermute | solution.py:21
